TPU v7x, 32 devices: a whole 2x2x4 slice. The times are simulated.
32 devices in a mesh: seq: 8 (over z, y), fsdp: 4 (over x, core).
Axes of the slice: x: 2, y: 2, z: 4, core: 2. Of those that a mesh axis runs over, the one named last changes fastest.
Arguments:
- inputs: bfloat16 [12288, 1536], P(('seq', 'fsdp')), may hold values from -15 to 15
- layer_norm_gain: float32 [1536], replicated, may hold values from 0.25 to 1.75
- layer_norm_bias: float32 [1536], replicated, may hold values from -4 to 4
- w_in: bfloat16 [1536, 3072], P('fsdp'), may hold values from -0.15625 to 0.15625
- dw_kernel: float32 [32, 1536], replicated, may hold values from -1 to 1
- bn_gain: float32 [1536], replicated, may hold values from 0.25 to 1.75
- bn_bias: float32 [1536], replicated, may hold values from -4 to 4
- cotangent: bfloat16 [12288, 1536], P(('seq', 'fsdp')), may hold values from -6 to 6
Outputs:
- output: bfloat16 [12288, 1536], P(('seq', 'fsdp'))
- input_gradient: bfloat16 [12288, 1536], P(('seq', 'fsdp'))
- grad_w_in: float32 [1536, 3072], P('fsdp')
- grad_kernel: float32 [32, 1536], replicated
- grad_bn_gain: float32 [1536], replicated
- grad_bn_bias: float32 [1536], replicated
- layer_norm_gain_gradient: float32 [1536], replicated
- grad_ln_bias: float32 [1536], replicated
All inputs are finite; a program needn't handle non-finite values.
Results may differ from a plain program's by a relative error of at most 0.012.
The roundings to bfloat16 on the way count: a program that leaves them out, or rounds other values in their place, can miss the bound.
Values may be sent and summed in bfloat16 or wider, within the bound.
No kernel may reach another device: no remote copies, remote signals or barrier semaphores. Data moves between devices by JAX's collectives and lax.ppermute only.
A program may use at most 128 MiB of HBM per device.

v0:
```python
import jax
import jax.numpy as jnp
from jax import lax
from jax.sharding import PartitionSpec as P

epsilon = 1e-05


def from_behind(block, axis, distance):
    devices = range(lax.axis_size(axis))
    route = [(i - distance, i) for i in devices if i - distance in devices]
    return lax.ppermute(block, axis, route)


def tree_sum(tree, axis):
    count = lax.axis_size(axis)
    if count & count - 1:
        return lax.psum(tree, axis)
    stride = 1
    while stride < count:
        route = [(i, i ^ stride) for i in range(count)]
        tree = jax.tree.map(lambda x: x + lax.ppermute(x, axis, route), tree)
        stride *= 2
    return tree


def on_device(
    inputs, layer_norm_gain, layer_norm_bias, w_in, dw_kernel, bn_gain, bn_bias, cotangent
):
    tok_rows = inputs.shape[0]
    features = inputs.shape[1]
    kernel_len = dw_kernel.shape[0]
    all_frames = tok_rows * lax.axis_size("seq") * lax.axis_size("fsdp")
    frames = inputs.astype(jnp.float32)
    row_mean = jnp.mean(frames, axis=-1, keepdims=True)
    centered_rows = frames - row_mean
    row_inverse_deviation = lax.rsqrt(
        jnp.mean(centered_rows * centered_rows, axis=-1, keepdims=True) + epsilon
    )
    standardized_input = centered_rows * row_inverse_deviation
    normalized_rows = (standardized_input * layer_norm_gain + layer_norm_bias).astype(jnp.bfloat16)
    full_weight = lax.all_gather(w_in, "fsdp", axis=0, tiled=True)
    hidden = jnp.dot(normalized_rows, full_weight, preferred_element_type=jnp.float32)
    value_part = hidden[:, :features]
    gate_sig = jax.nn.sigmoid(hidden[:, features:])
    glu = (value_part * gate_sig).astype(jnp.bfloat16)
    past_rim = from_behind(glu[tok_rows - (kernel_len - 1) :], ("seq", "fsdp"), 1)
    padded_glu = jnp.concatenate([past_rim, glu], axis=0).astype(jnp.float32)
    conv_out = jnp.zeros((tok_rows, features), jnp.float32)
    for offset in range(kernel_len):
        conv_out = (
            conv_out
            + dw_kernel[offset]
            * padded_glu[kernel_len - 1 - offset : kernel_len - 1 - offset + tok_rows]
        )
    chan_mean = tree_sum(jnp.sum(conv_out, axis=0), ("seq", "fsdp")) / all_frames
    conv_centred = conv_out - chan_mean
    chan_var = tree_sum(jnp.sum(conv_centred * conv_centred, axis=0), ("seq", "fsdp")) / all_frames
    bn_rstd = lax.rsqrt(chan_var + epsilon)
    chat = conv_centred * bn_rstd
    z_value = chat * bn_gain + bn_bias
    z_sig = jax.nn.sigmoid(z_value)
    output = (z_value * z_sig).astype(jnp.bfloat16)
    grad_z = cotangent.astype(jnp.float32) * z_sig * (1.0 + z_value * (1.0 - z_sig))
    grad_bn_bias, grad_bn_gain = tree_sum(
        (jnp.sum(grad_z, axis=0), jnp.sum(grad_z * chat, axis=0)), ("seq", "fsdp")
    )
    grad_conv = (
        bn_gain * bn_rstd * (grad_z - grad_bn_bias / all_frames - chat * grad_bn_gain / all_frames)
    )
    future_rim = from_behind(grad_conv[: kernel_len - 1], ("seq", "fsdp"), -1)
    padded_grad = jnp.concatenate([grad_conv, future_rim], axis=0)
    grad_glu = jnp.zeros((tok_rows, features), jnp.float32)
    kernel_rows = []
    for offset in range(kernel_len):
        grad_glu = grad_glu + dw_kernel[offset] * padded_grad[offset : offset + tok_rows]
        kernel_rows.append(
            jnp.sum(
                grad_conv
                * padded_glu[kernel_len - 1 - offset : kernel_len - 1 - offset + tok_rows],
                axis=0,
            )
        )
    kernel_portion = jnp.stack(kernel_rows, axis=0)
    grad_value = grad_glu * gate_sig
    grad_gate = grad_glu * value_part * gate_sig * (1.0 - gate_sig)
    grad_hidden = jnp.concatenate([grad_value, grad_gate], axis=1).astype(jnp.bfloat16)
    normalized_gradient = lax.dot_general(
        grad_hidden, full_weight, (((1,), (1,)), ((), ())), preferred_element_type=jnp.float32
    )
    grad_kernel, layer_norm_gain_gradient, grad_ln_bias = tree_sum(
        (
            kernel_portion,
            jnp.sum(normalized_gradient * standardized_input, axis=0),
            jnp.sum(normalized_gradient, axis=0),
        ),
        ("seq", "fsdp"),
    )
    rescaled_rows = normalized_gradient * layer_norm_gain
    input_gradient = row_inverse_deviation * (
        rescaled_rows
        - jnp.mean(rescaled_rows, axis=-1, keepdims=True)
        - standardized_input * jnp.mean(rescaled_rows * standardized_input, axis=-1, keepdims=True)
    )
    row_share = lax.psum_scatter(
        lax.dot_general(
            normalized_rows,
            grad_hidden,
            (((0,), (0,)), ((), ())),
            preferred_element_type=jnp.float32,
        ),
        "fsdp",
        scatter_dimension=0,
        tiled=True,
    )
    grad_w_in = lax.psum(row_share, "seq")
    return (
        output,
        input_gradient.astype(jnp.bfloat16),
        grad_w_in,
        grad_kernel,
        grad_bn_gain,
        grad_bn_bias,
        layer_norm_gain_gradient,
        grad_ln_bias,
    )


def solution(mesh):
    placed = (
        P(("seq", "fsdp"), None),
        P(),
        P(),
        P("fsdp", None),
        P(),
        P(),
        P(),
        P(("seq", "fsdp"), None),
    )
    return jax.shard_map(
        on_device,
        mesh=mesh,
        in_specs=placed,
        out_specs=(
            P(("seq", "fsdp"), None),
            P(("seq", "fsdp"), None),
            P("fsdp", None),
            P(),
            P(),
            P(),
            P(),
            P(),
        ),
        check_vma=False,
    )
```

profile of v0, /device:TPU:0, one launch (start us, length us, event | category | flops | bytes accessed | tf_op | source)
XLA Modules:
  0.0 560.9 jit_solution(14859436354774125420)
XLA Ops:
  7.3 0.7 all-gather.2.cloned.1.call-update
  9.3 67.3 %all-gather.2.cloned.1.call-done = bf16[1536,3072]{1,0:T(8,128)(2,1)} async-done(((bf16[384,3072]{1,0:T(8,128)(2,1)}), bf16[1536,3072]{1,0:T(8,128)(2,1)}) %all-gather.2.cloned.1.call-update) | async-done | bytes 9437200 | tf_op jit(solution)/shard_map/all_gather | solution.py:42
  76.6 6.7 %fusion.114 = f32[384,3072]{1,0:T(8,128)S(1)} fusion(bf16[1536,3072]{1,0:T(8,128)(2,1)} %all-gather.2.cloned.1.call-done, bf16[384,1536]{1,0:T(8,128)(2,1)S(1)} %copy-done.2, f32[1536]{0:T(1024)S(1)} %copy-done.10, f32[1536]{0:T(1024)S(1)} %copy-done.9, f32[384]{0:T(512)S(1)} %add_rsqrt_fusion.1, f32[384]{0:T(512)S(1)} %broadcast_multiply_fusion.3), kind=kOutput, calls=%fused_computation.258 | convolution fusion | flops 3627417600 | bytes 15350784 | tf_op jit(solution)/shard_map/dot_general | solution.py:43
  83.9 1.5 copy-done
  85.5 2.2 collective-permute-start
  87.9 0.7 collective-permute-done
  88.9 9.4 %fusion.119 = (f32[1536]{0:T(1024)S(1)}, f32[384,1536]{1,0:T(8,128)S(1)}) fusion(f32[415,1536]{1,0:T(8,128)S(1)} %maximum_convert_fusion, f32[1536]{0:T(1024)S(1)} %get-tuple-element.76, f32[1536]{0:T(1024)S(1)} %get-tuple-element.77, f32[1536]{0:T(1024)S(1)} %get-tuple-element.47, f32[1536]{0:T(1024)S(1)} %get-tuple-element.48, ...), kind=kLoop, calls=%fused_computation.261 | loop fusion | flops 37747200 | bytes 78059520 | tf_op jit(solution)/shard_map/reduce_sum | solution.py:56
  98.4 0.9 collective-permute-start.1
  99.3 0.8 collective-permute-done.1
  100.2 2.6 collective-permute-start.2
  102.8 1.6 collective-permute-done.2
  104.4 4.1 collective-permute-start.3
  108.5 1.6 collective-permute-done.3
  110.2 2.9 collective-permute-start.4
  113.1 1.6 collective-permute-done.4
  114.7 2.9 collective-permute-start.5
  117.7 1.6 collective-permute-done.5
  119.7 1.2 collective-permute-done.6
  120.8 3.6 collective-permute-done.7
  124.5 1.1 collective-permute-start.8
  125.6 2.6 collective-permute-done.8
  128.1 2.0 collective-permute-start.9
  130.1 1.6 collective-permute-done.9
  131.8 2.9 collective-permute-start.10
  134.7 1.6 collective-permute-done.10
  136.4 2.5 fusion.116
  140.2 1.9 collective-permute-start.17
  142.1 1.6 collective-permute-done.12
  143.7 1.1 collective-permute-start.13
  144.8 0.9 collective-permute-start.18
  145.7 1.6 collective-permute-done.13
  147.4 2.0 collective-permute-start.14
  149.9 1.1 collective-permute-done.14
  151.0 2.9 collective-permute-start.15
  153.9 1.6 collective-permute-start.20
  156.2 2.3 collective-permute-done.20
  158.5 7.1 %multiply_reduce_fusion = (f32[1536]{0:T(1024)S(1)}, f32[1536]{0:T(1024)S(1)}, f32[1536]{0:T(1024)S(1)}, f32[1536]{0:T(1024)S(1)}, f32[1536]{0:T(1024)S(1)}, /*i...) fusion(f32[415,1536]{1,0:T(8,128)S(1)} %maximum_convert_fusion,, ...), kind=kLoop, calls=%fused_computation.169 | loop fusion | flops 31822848 | bytes 48519168 | tf_op jit(solution)/shard_map/reduce_sum | solution.py:78
  165.6 1.4 copy-done.1
  167.0 1.5 collective-permute-start.21
  168.5 1.9 collective-permute-done.21
  170.3 40.4 %multiply_convert_fusion.1 = (bf16[384,1536]{1,0:T(8,128)(2,1)S(1)}, f32[384,1536]{1,0:T(8,128)}) fusion(f32[384,3072]{1,0:T(8,128)} %copy-done, f32[31,1536]{1,0:T(8,128)S(1)} %collective-permute-done.21, f32[384,1536]{1,0:T(8,128)} %copy-done.1, f32[1536]{0:T(1024)S(1)} %get-tuple-element.76, f32[1536]{0:T(1024)S(1)} %get-tuple-element.77, ...), kind=kLoop, calls=%fused_computation.202 | loop fusion | flops 58392576 | bytes 8644608 | tf_op jit(solution)/shard_map/convert
  210.8 4.4 multiply_convert_fusion
  215.3 1.0 copy-done.7
  216.3 9.4 %fusion.109 = f32[1536,3072]{1,0:T(8,128)} fusion(bf16[384,1536]{1,0:T(8,128)(2,1)S(1)} %multiply_convert_fusion, bf16[384,1536]{1,0:T(8,128)(2,1)S(1)} %get-tuple-element.79, bf16[384,1536]{1,0:T(8,128)(2,1)S(1)} %copy-done.3, f32[1536]{0:T(1024)S(1)} %copy-done.10, f32[1536]{0:T(1024)S(1)} %copy-done.9, f32[384]{0:T(512)S(1)} %add_rsqrt_fusion.1, ...), kind=kOutput, calls=%fused_computation.214 | convolution fusion | flops 3632136192 | bytes 22428672 | tf_op jit(solution)/shard_map/dot_general | solution.py:106
  226.0 140.8 %reduce-scatter.2.cloned.1.call-done = f32[384,3072]{1,0:T(8,128)} async-done(((f32[1536,3072]{1,0:T(8,128)}), f32[384,3072]{1,0:T(8,128)}) %reduce-scatter.2.cloned.1.call-update) | async-done | bytes 4718608 | tf_op jit(solution)/shard_map/reduce_scatter | solution.py:105
  366.8 5.4 multiply_reduce_fusion.18
  373.1 1.4 collective-permute-done.22
  374.9 6.6 %collective-permute-done.23 = f32[32,1536]{1,0:T(8,128)S(1)} collective-permute-done((f32[32,1536]{1,0:T(8,128)S(1)}, f32[32,1536]{1,0:T(8,128)S(1)}, u32[]{:S(2)}, u32[]{:S(2)}) %collective-permute-start.23) | collective-permute-done | bytes 196640 | tf_op jit(solution)/shard_map/ppermute | solution.py:22
  381.6 1.5 collective-permute-start.24
  383.1 9.1 %fusion.12 = (f32[1536]{0:T(1024)S(1)}, f32[384]{0:T(512)S(1)}, f32[384]{0:T(512)S(1)}, f32[1536]{0:T(1024)S(1)}, f32[384,1536]{1,0:T(8,128)S(1)}) fusion(bf16[384,1536]{1,0:T(8,128)(2,1)} %param.8, f32[384]{0:T(512)S(1)} %add_rsqrt_fusion.1, f32[384]{0:T(512)S(1)} %broadcast_multiply_fusion.3, f32[1536]{0:T(1024)S(1)} %copy-done.9, ...), kind=kOutput, calls=%fused_computation.44 | convolution fusion | flops 3634491392 | bytes 15360000 | tf_op jit(solution)/shard_map/dot_general | solution.py:88
  394.0 1.5 collective-permute-start.33
  395.5 1.6 collective-permute-done.28
  397.7 1.5 collective-permute-start.34
  399.2 1.6 collective-permute-done.29
  400.8 1.5 collective-permute-start.30
  402.9 1.5 collective-permute-start.25
  404.4 2.2 collective-permute-done.30
  407.1 2.4 collective-permute-start.36
  409.5 17.2 %collective-permute-done.25 = f32[32,1536]{1,0:T(8,128)S(1)} collective-permute-done((f32[32,1536]{1,0:T(8,128)S(1)}, f32[32,1536]{1,0:T(8,128)S(1)}, u32[]{:S(2)}, u32[]{:S(2)}) %collective-permute-start.25) | collective-permute-done | bytes 196640 | tf_op jit(solution)/shard_map/ppermute | solution.py:22
  427.3 1.8 fusion.11
  430.3 9.8 %collective-permute-done.26 = f32[32,1536]{1,0:T(8,128)S(1)} collective-permute-done((f32[32,1536]{1,0:T(8,128)S(1)}, f32[32,1536]{1,0:T(8,128)S(1)}, u32[]{:S(2)}, u32[]{:S(2)}) %collective-permute-start.26) | collective-permute-done | bytes 196640 | tf_op jit(solution)/shard_map/ppermute | solution.py:22
  440.1 0.7 add.434
  440.8 108.5 %all-reduce.2.cloned.1.call-done = f32[384,3072]{1,0:T(8,128)} async-done(((f32[384,3072]{1,0:T(8,128)}), f32[384,3072]{1,0:T(8,128)}) %all-reduce.2.cloned.1.call-update) | async-done | bytes 4718608 | tf_op jit(solution)/shard_map/psum | solution.py:116
  549.3 5.1 copy.17
  (138 shorter events, 12.2 us)
Async XLA Ops:
  7.2 0.9 copy-start.8
  7.2 1.4 copy-start.2
  7.2 69.4 %copy-start.9 = (f32[1536]{0:T(1024)S(1)}, f32[1536]{0:T(1024)}, u32[]{:S(2)}) copy-start(f32[1536]{0:T(1024)} %param.9) | copy-start | bytes 18436
  7.2 69.4 %copy-start.10 = (f32[1536]{0:T(1024)S(1)}, f32[1536]{0:T(1024)}, u32[]{:S(2)}) copy-start(f32[1536]{0:T(1024)} %param.10) | copy-start | bytes 18436
  7.2 69.4 %all-gather.2.cloned.1.call-start = ((), (), s32[]{:S(2)}) async-start(), calls=%async_computation.1 | async-start | bytes 11796480 | tf_op jit(solution)/shard_map/all_gather | solution.py:42
  7.9 358.8 %reduce-scatter.2.cloned.1.call-start = ((), (), s32[]{:S(2)}) async-start(), calls=%async_computation.2 | async-start | bytes 23592960 | tf_op jit(solution)/shard_map/reduce_scatter | solution.py:105
  83.3 2.2 copy-start
  85.5 3.1 collective-permute-start
  98.4 38.0 %copy-start.11 = (f32[1536]{0:T(1024)S(1)}, f32[1536]{0:T(1024)}, u32[]{:S(2)}) copy-start(f32[1536]{0:T(1024)} %param.13) | copy-start | bytes 18436
  98.4 38.0 %copy-start.5 = (bf16[384,1536]{1,0:T(8,128)(2,1)S(1)}, bf16[384,1536]{1,0:T(8,128)(2,1)}, u32[]{:S(2)}) copy-start(bf16[384,1536]{1,0:T(8,128)(2,1)} %param.15) | copy-start | bytes 3538948
  98.4 38.0 %copy-start.12 = (f32[1536]{0:T(1024)S(1)}, f32[1536]{0:T(1024)}, u32[]{:S(2)}) copy-start(f32[1536]{0:T(1024)} %param.14) | copy-start | bytes 18436
  98.4 1.8 collective-permute-start.1
  100.2 4.3 collective-permute-start.2
  104.4 5.7 %collective-permute-start.3 = (f32[1536]{0:T(1024)S(1)}, f32[1536]{0:T(1024)S(1)}, u32[]{:S(2)}, u32[]{:S(2)}) collective-permute-start(f32[1536]{0:T(1024)S(1)} %add.374), channel_id=1, source_target_pairs={{0,4},{1,5},{2,6},{3,7},{4,0},{5,1},{6,2},{7,3},{8,12},{9,13},{10,... | collective-permute-start | bytes 18440 | tf_op jit(solution)/shard_map/ppermute | solution.py:22
  110.2 4.6 collective-permute-start.4
  114.7 4.6 collective-permute-start.5
  119.6 1.2 collective-permute-start.6
  120.8 3.7 collective-permute-start.7
  124.5 3.7 collective-permute-start.8
  128.1 3.7 collective-permute-start.9
  131.8 4.6 collective-permute-start.10
  138.9 1.2 collective-permute-start.11
  138.9 1.3 collective-permute-start.16
  140.0 3.7 collective-permute-start.12
  140.2 4.6 collective-permute-start.17
  143.7 3.7 collective-permute-start.13
  144.8 4.6 collective-permute-start.18
  147.4 3.7 collective-permute-start.14
  149.4 4.6 collective-permute-start.19
  151.0 4.5 collective-permute-start.15
  153.9 4.6 collective-permute-start.20
  158.5 7.1 %copy-start.13 = (f32[1536]{0:T(1024)}, f32[1536]{0:T(1024)S(1)}, u32[]{:S(2)}) copy-start(f32[1536]{0:T(1024)S(1)} %add.398) | copy-start | bytes 18436
  165.6 1.4 copy-start.1
  167.0 3.3 collective-permute-start.21
  210.8 4.5 copy-start.6
  210.8 5.5 copy-start.3
  215.3 1.0 copy-start.7
  225.7 323.6 %all-reduce.2.cloned.1.call-start = ((), (), s32[]{:S(2)}) async-start(), calls=%async_computation.3 | async-start | bytes 9437184 | tf_op jit(solution)/shard_map/psum | solution.py:116
  373.0 1.5 collective-permute-start.22
  374.6 7.0 %collective-permute-start.23 = (f32[32,1536]{1,0:T(8,128)S(1)}, f32[32,1536]{1,0:T(8,128)S(1)}, u32[]{:S(2)}, u32[]{:S(2)}) collective-permute-start(f32[32,1536]{1,0:T(8,128)S(1)} %add.430), channel_id=1, source_target_pairs={{0,2},{1,3},{2,0},{3,1},{4,6},{5,7},{6,4},{7,5},{8,10},{9,11},{10,... | collective-permute-start | bytes 589832 | tf_op jit(solution)/shard_map/ppermute | solution.py:22
  381.6 45.7 %copy-start.4 = (bf16[384,1536]{1,0:T(8,128)(2,1)S(1)}, bf16[384,1536]{1,0:T(8,128)(2,1)}, u32[]{:S(2)}) copy-start(bf16[384,1536]{1,0:T(8,128)(2,1)} %param.8) | copy-start | bytes 3538948
  381.6 21.3 %collective-permute-start.24 = (f32[32,1536]{1,0:T(8,128)S(1)}, f32[32,1536]{1,0:T(8,128)S(1)}, u32[]{:S(2)}, u32[]{:S(2)}) collective-permute-start(f32[32,1536]{1,0:T(8,128)S(1)} %add.431), channel_id=1, source_target_pairs={{0,4},{1,5},{2,6},{3,7},{4,0},{5,1},{6,2},{7,3},{8,12},{9,13},{10,... | collective-permute-start | bytes 589832 | tf_op jit(solution)/shard_map/ppermute | solution.py:22
  392.2 1.2 collective-permute-start.27
  392.3 1.7 collective-permute-start.32
  393.5 3.7 collective-permute-start.28
  394.0 3.7 collective-permute-start.33
  397.1 3.7 collective-permute-start.29
  397.7 4.6 collective-permute-start.34
  400.8 5.8 %collective-permute-start.30 = (f32[1536]{0:T(1024)S(1)}, f32[1536]{0:T(1024)S(1)}, u32[]{:S(2)}, u32[]{:S(2)}) collective-permute-start(f32[1536]{0:T(1024)S(1)} %add.437), channel_id=1, source_target_pairs={{0,8},{1,9},{2,10},{3,11},{4,12},{5,13},{6,14},{7,15},{8,0},{9,1},... | collective-permute-start | bytes 18440 | tf_op jit(solution)/shard_map/ppermute | solution.py:22
  402.3 4.8 collective-permute-start.35
  402.9 23.9 %collective-permute-start.25 = (f32[32,1536]{1,0:T(8,128)S(1)}, f32[32,1536]{1,0:T(8,128)S(1)}, u32[]{:S(2)}, u32[]{:S(2)}) collective-permute-start(f32[32,1536]{1,0:T(8,128)S(1)} %add.432), channel_id=1, source_target_pairs={{0,8},{1,9},{2,10},{3,11},{4,12},{5,13},{6,14},{7,15},{8,0},{9,1},... | collective-permute-start | bytes 589832 | tf_op jit(solution)/shard_map/ppermute | solution.py:22
  406.6 22.5 %collective-permute-start.31 = (f32[1536]{0:T(1024)S(1)}, f32[1536]{0:T(1024)S(1)}, u32[]{:S(2)}, u32[]{:S(2)}) collective-permute-start(f32[1536]{0:T(1024)S(1)} %add.438), channel_id=1, source_target_pairs={{0,16},{1,17},{2,18},{3,19},{4,20},{5,21},{6,22},{7,23},{8,24},{9,... | collective-permute-start | bytes 18440 | tf_op jit(solution)/shard_map/ppermute | solution.py:22
  407.1 22.6 %collective-permute-start.36 = (f32[1536]{0:T(1024)S(1)}, f32[1536]{0:T(1024)S(1)}, u32[]{:S(2)}, u32[]{:S(2)}) collective-permute-start(f32[1536]{0:T(1024)S(1)} %add.443), channel_id=1, source_target_pairs={{0,16},{1,17},{2,18},{3,19},{4,20},{5,21},{6,22},{7,23},{8,24},{9,... | collective-permute-start | bytes 18440 | tf_op jit(solution)/shard_map/ppermute | solution.py:22
  426.8 13.4 %collective-permute-start.26 = (f32[32,1536]{1,0:T(8,128)S(1)}, f32[32,1536]{1,0:T(8,128)S(1)}, u32[]{:S(2)}, u32[]{:S(2)}) collective-permute-start(f32[32,1536]{1,0:T(8,128)S(1)} %add.433), channel_id=1, source_target_pairs={{0,16},{1,17},{2,18},{3,19},{4,20},{5,21},{6,22},{7,23},{8,24},{9,... | collective-permute-start | bytes 589832 | tf_op jit(solution)/shard_map/ppermute | solution.py:22
Sparse Core Ops, SparseCore 0:
  9.6 66.9 all-gather.1
  225.8 140.8 reduce-scatter.1
  370.8 178.4 all-reduce.1
where the time goes:
time: 561 us
  waiting for transfers between devices  387 us (69%)
  other arithmetic  75.8 us (14%)
  starting transfers between devices  48.7 us (9%)
  matrix products  25.2 us (4%)
  between operations  14.3 us (3%)
  local copies, waits for them, and re-layouts  10.4 us (2%)
    reduce_scatter x1, waiting for transfers between devices, on_device(): lax.psum_scatter(lax.dot_general(normalized_rows, grad_hidden, (((0,), (0...  141 us
    psum x1, waiting for transfers between devices, on_device(): grad_w_in = lax.psum(row_share, 'seq')  109 us
    all_gather x1, waiting for transfers between devices, on_device(): full_weight = lax.all_gather(w_in, 'fsdp', axis=0, tiled=True)  67.3 us
    ppermute x35, waiting for transfers between devices, tree_sum(): tree = jax.tree.map(lambda x: x + lax.ppermute(x, axis, route), tree)  66.7 us
    another operation x2, other arithmetic  44.9 us
    ppermute x35, starting transfers between devices, tree_sum(): tree = jax.tree.map(lambda x: x + lax.ppermute(x, axis, route), tree)  44.7 us
    reduce_sum x2, other arithmetic, on_device(): jnp.sum(grad_conv * padded_glu[kernel_len - 1 - offset:kernel_len - 1 - o...  12.6 us
  transfers between devices with their start and end apart: 40, of which 30 were waited for; matrix products, arithmetic and copies ran while one was open for 4% of the time, Pallas kernels for 0%

commit v1 on v0

--- a/solution.py
+++ b/solution.py
@@ -1,9 +1,44 @@
+import functools
 import jax
 import jax.numpy as jnp
 from jax import lax
 from jax.sharding import PartitionSpec as P
 
 epsilon = 1e-05
+
+
+def launch_the_screen(xs, axis_key, which_dim):
+    val2, item_now, before = (
+        lax.axis_size(axis_key),
+        lax.axis_index(axis_key),
+        xs.shape[which_dim],
+    )
+    seen = []
+    for nth, t in enumerate(xs.shape):
+        seen.append(t * val2 if nth == which_dim else t)
+    f_now = jnp.zeros(seen, xs.dtype)
+    local_part = w1 = xs
+    u_next = lax.dynamic_update_slice_in_dim(f_now, xs, item_now * before, axis=which_dim)
+    for s in range(1, val2 // 2 + 1):
+        items = []
+        for nth in range(val2):
+            items.append((nth, (nth + 1) % val2))
+        local_part = lax.ppermute(local_part, axis_key, items)
+        u_next = lax.dynamic_update_slice_in_dim(
+            u_next, local_part, (item_now - s) % val2 * before, axis=which_dim
+        )
+        if 2 * s < val2:
+            pile = []
+            for nth in range(val2):
+                pile.append((nth, (nth - 1) % val2))
+            w1 = lax.ppermute(w1, axis_key, pile)
+            u_next = lax.dynamic_update_slice_in_dim(
+                u_next, w1, (item_now + s) % val2 * before, axis=which_dim
+            )
+    return u_next
+
+
+_play_stages_all = functools.partial(launch_the_screen, axis_key="fsdp", which_dim=0)
 
 
 def from_behind(block, axis, distance):
@@ -39,7 +74,7 @@
     )
     standardized_input = centered_rows * row_inverse_deviation
     normalized_rows = (standardized_input * layer_norm_gain + layer_norm_bias).astype(jnp.bfloat16)
-    full_weight = lax.all_gather(w_in, "fsdp", axis=0, tiled=True)
+    full_weight = _play_stages_all(w_in)
     hidden = jnp.dot(normalized_rows, full_weight, preferred_element_type=jnp.float32)
     value_part = hidden[:, :features]
     gate_sig = jax.nn.sigmoid(hidden[:, features:])

time: 561 us -> 574 us (1.023)
  local copies, waits for them, and re-layouts: 10.4 us -> 19.3 us
  starting transfers between devices: 48.7 us -> 55.8 us
    all_gather x1 -> x0, waiting for transfers between devices: 67.3 us -> none  [on_device(): full_weight = lax.all_gather(w_in, 'fsdp', axis=0, tiled=True)]
    ppermute x0 -> x3, waiting for transfers between devices: none -> 66.8 us  [the longest x2 66.8 us: launch_the_screen(): local_part = lax.ppermute(local_part, axis_key, items)]
  transfers between devices with their start and end apart: 40 -> 42, of which waited for: 30 -> 29; matrix products, arithmetic and copies ran while one was open for 4% -> 5% of each run, Pallas kernels for 0% -> 0%
where the time goes in v1:
time: 574 us; the launch traced here: 573 us
  waiting for transfers between devices  384 us (67%)
  other arithmetic  77 us (13%)
  starting transfers between devices  55.8 us (10%)
  matrix products  22.6 us (4%)
  local copies, waits for them, and re-layouts  19.3 us (3%)
  between operations  14.7 us (3%)
    reduce_scatter x1, waiting for transfers between devices, on_device(): lax.psum_scatter(lax.dot_general(normalized_rows, grad_hidden, (((0,), (0...  141 us
    psum x1, waiting for transfers between devices, on_device(): grad_w_in = lax.psum(row_share, 'seq')  109 us
    ppermute x2, waiting for transfers between devices, launch_the_screen(): local_part = lax.ppermute(local_part, axis_key, items)  66.8 us
    ppermute x35, waiting for transfers between devices, tree_sum(): tree = jax.tree.map(lambda x: x + lax.ppermute(x, axis, route), tree)  65.9 us
    another operation x2, other arithmetic  44.8 us
    ppermute x35, starting transfers between devices, tree_sum(): tree = jax.tree.map(lambda x: x + lax.ppermute(x, axis, route), tree)  44.3 us
    reduce_sum x2, other arithmetic, on_device(): jnp.sum(grad_conv * padded_glu[kernel_len - 1 - offset:kernel_len - 1 - o...  12.5 us
  transfers between devices with their start and end apart: 42, of which 29 were waited for; matrix products, arithmetic and copies ran while one was open for 5% of the time, Pallas kernels for 0%

profile of v1, /device:TPU:0, one launch (start us, length us, event | category | flops | bytes accessed | tf_op | source)
XLA Modules:
  0.0 573.4 jit_solution(12138351405461055186)
XLA Ops:
  7.7 2.0 collective-permute-start.1
  9.7 49.3 %collective-permute-done = bf16[384,3072]{1,0:T(8,128)(2,1)S(1)} collective-permute-done((bf16[384,3072]{1,0:T(8,128)(2,1)}, bf16[384,3072]{1,0:T(8,128)(2,1)S(1)}, u32[]{:S(2)}, u32[]{:S(2)}) %collective-permute-start) | collective-permute-done | bytes 2359328 | tf_op jit(solution)/shard_map/ppermute | solution.py:26
  59.0 2.6 collective-permute-start.2
  61.6 2.0 slice_reduce_fusion.31
  63.7 1.5 convert_reduce_fusion
  65.6 1.2 broadcast_in_dim.2
  67.9 1.9 constant_dynamic-update-slice_fusion.1
  69.9 17.5 %collective-permute-done.2 = bf16[384,3072]{1,0:T(8,128)(2,1)} collective-permute-done((bf16[384,3072]{1,0:T(8,128)(2,1)S(1)}, bf16[384,3072]{1,0:T(8,128)(2,1)}, u32[]{:S(2)}, u32[]{:S(2)}) %collective-permute-start.2) | collective-permute-done | bytes 2359328 | tf_op jit(solution)/shard_map/ppermute | solution.py:26
  87.4 1.9 constant_dynamic-update-slice_fusion
  89.4 4.1 fusion.114
  94.1 1.5 copy-done
  95.7 4.5 collective-permute-start.3
  100.2 1.5 slice_reduce_fusion.30
  102.1 9.4 %fusion.119 = (f32[1536]{0:T(1024)S(1)}, f32[384,1536]{1,0:T(8,128)S(1)}) fusion(f32[415,1536]{1,0:T(8,128)S(1)} %maximum_convert_fusion, f32[1536]{0:T(1024)S(1)} %get-tuple-element.76, f32[1536]{0:T(1024)S(1)} %get-tuple-element.77, f32[1536]{0:T(1024)S(1)} %get-tuple-element.47, f32[1536]{0:T(1024)S(1)} %get-tuple-element.48, ...), kind=kLoop, calls=%fused_computation.265 | loop fusion | flops 37747200 | bytes 78059520 | tf_op jit(solution)/shard_map/reduce_sum | solution.py:91
  111.6 2.6 collective-permute-start.4
  115.1 2.5 collective-permute-start.5
  117.6 1.6 collective-permute-done.5
  119.2 1.2 collective-permute-start.6
  120.4 2.5 collective-permute-done.6
  122.9 2.1 collective-permute-start.7
  125.0 1.6 collective-permute-done.7
  126.6 3.0 collective-permute-start.8
  129.7 1.6 collective-permute-done.8
  131.7 1.2 collective-permute-done.9
  132.8 1.8 collective-permute-start.10
  134.6 1.9 collective-permute-done.10
  137.4 2.7 collective-permute-done.11
  140.1 1.9 collective-permute-start.12
  142.1 1.7 collective-permute-done.12
  143.8 2.9 collective-permute-start.13
  146.7 1.6 collective-permute-done.13
  148.4 2.5 fusion.116
  152.0 1.8 collective-permute-start.15
  154.1 1.6 collective-permute-done.15
  159.3 1.9 collective-permute-start.17
  163.0 2.9 collective-permute-start.18
  165.9 1.6 collective-permute-start.23
  168.2 2.3 collective-permute-done.23
  170.5 7.1 %multiply_reduce_fusion = (f32[1536]{0:T(1024)S(1)}, f32[1536]{0:T(1024)S(1)}, f32[1536]{0:T(1024)S(1)}, f32[1536]{0:T(1024)S(1)}, f32[1536]{0:T(1024)S(1)}, /*i...) fusion(f32[415,1536]{1,0:T(8,128)S(1)} %maximum_convert_fusion,, ...), kind=kLoop, calls=%fused_computation.169 | loop fusion | flops 31822848 | bytes 48519168 | tf_op jit(solution)/shard_map/reduce_sum | solution.py:113
  177.6 1.4 copy-done.1
  179.0 1.5 collective-permute-start.24
  180.5 1.8 collective-permute-done.24
  182.3 40.4 %multiply_convert_fusion.1 = (bf16[384,1536]{1,0:T(8,128)(2,1)S(1)}, f32[384,1536]{1,0:T(8,128)}) fusion(f32[384,3072]{1,0:T(8,128)} %copy-done, f32[31,1536]{1,0:T(8,128)S(1)} %collective-permute-done.24, f32[384,1536]{1,0:T(8,128)} %copy-done.1, f32[1536]{0:T(1024)S(1)} %get-tuple-element.76, f32[1536]{0:T(1024)S(1)} %get-tuple-element.77, ...), kind=kLoop, calls=%fused_computation.202 | loop fusion | flops 58392576 | bytes 8644608 | tf_op jit(solution)/shard_map/convert
  222.8 4.4 multiply_convert_fusion
  228.2 9.4 %fusion.109 = f32[1536,3072]{1,0:T(8,128)} fusion(bf16[384,1536]{1,0:T(8,128)(2,1)S(1)} %multiply_convert_fusion, bf16[384,1536]{1,0:T(8,128)(2,1)S(1)} %get-tuple-element.79, bf16[384,1536]{1,0:T(8,128)(2,1)S(1)} %copy-done.3, f32[1536]{0:T(1024)S(1)} %copy-done.11, f32[1536]{0:T(1024)S(1)} %copy-done.10, f32[384]{0:T(512)S(1)} %add_rsqrt_fusion.1, ...), kind=kOutput, calls=%fused_computation.214 | convolution fusion | flops 3632136192 | bytes 22428672 | tf_op jit(solution)/shard_map/dot_general | solution.py:141
  238.0 140.9 %reduce-scatter.2.cloned.1.call-done = f32[384,3072]{1,0:T(8,128)} async-done(((f32[1536,3072]{1,0:T(8,128)}), f32[384,3072]{1,0:T(8,128)}) %reduce-scatter.2.cloned.1.call-update) | async-done | bytes 4718608 | tf_op jit(solution)/shard_map/reduce_scatter | solution.py:140
  378.9 5.4 multiply_reduce_fusion.18
  385.2 1.4 collective-permute-done.25
  387.1 6.6 %collective-permute-done.26 = f32[32,1536]{1,0:T(8,128)S(1)} collective-permute-done((f32[32,1536]{1,0:T(8,128)S(1)}, f32[32,1536]{1,0:T(8,128)S(1)}, u32[]{:S(2)}, u32[]{:S(2)}) %collective-permute-start.26) | collective-permute-done | bytes 196640 | tf_op jit(solution)/shard_map/ppermute | solution.py:57
  393.8 1.5 collective-permute-start.27
  395.3 9.1 %fusion.12 = (f32[1536]{0:T(1024)S(1)}, f32[384]{0:T(512)S(1)}, f32[384]{0:T(512)S(1)}, f32[1536]{0:T(1024)S(1)}, f32[384,1536]{1,0:T(8,128)S(1)}) fusion(bf16[384,1536]{1,0:T(8,128)(2,1)} %param.8, f32[384]{0:T(512)S(1)} %add_rsqrt_fusion.1, f32[384]{0:T(512)S(1)} %broadcast_multiply_fusion.3, f32[1536]{0:T(1024)S(1)} %copy-done.10, ...), kind=kOutput, calls=%fused_computation.44 | convolution fusion | flops 3634491392 | bytes 15360000 | tf_op jit(solution)/shard_map/dot_general | solution.py:123
  406.2 1.5 collective-permute-start.36
  407.7 1.6 collective-permute-done.31
  409.9 1.5 collective-permute-start.37
  411.3 1.6 collective-permute-done.32
  413.0 1.5 collective-permute-start.33
  415.1 1.5 collective-permute-start.28
  416.6 2.2 collective-permute-done.33
  419.3 2.4 collective-permute-start.39
  421.7 17.2 %collective-permute-done.28 = f32[32,1536]{1,0:T(8,128)S(1)} collective-permute-done((f32[32,1536]{1,0:T(8,128)S(1)}, f32[32,1536]{1,0:T(8,128)S(1)}, u32[]{:S(2)}, u32[]{:S(2)}) %collective-permute-start.28) | collective-permute-done | bytes 196640 | tf_op jit(solution)/shard_map/ppermute | solution.py:57
  439.5 1.8 fusion.11
  442.5 9.8 %collective-permute-done.29 = f32[32,1536]{1,0:T(8,128)S(1)} collective-permute-done((f32[32,1536]{1,0:T(8,128)S(1)}, f32[32,1536]{1,0:T(8,128)S(1)}, u32[]{:S(2)}, u32[]{:S(2)}) %collective-permute-start.29) | collective-permute-done | bytes 196640 | tf_op jit(solution)/shard_map/ppermute | solution.py:57
  453.0 108.5 %all-reduce.2.cloned.1.call-done = f32[384,3072]{1,0:T(8,128)} async-done(((f32[384,3072]{1,0:T(8,128)}), f32[384,3072]{1,0:T(8,128)}) %all-reduce.2.cloned.1.call-update) | async-done | bytes 4718608 | tf_op jit(solution)/shard_map/psum | solution.py:151
  561.5 5.1 copy.21
  (148 shorter events, 21.1 us)
Async XLA Ops:
  7.2 58.0 %copy-start.2 = (bf16[384,1536]{1,0:T(8,128)(2,1)S(1)}, bf16[384,1536]{1,0:T(8,128)(2,1)}, u32[]{:S(2)}) copy-start(bf16[384,1536]{1,0:T(8,128)(2,1)} %param.8) | copy-start | bytes 3538948
  7.2 371.7 %reduce-scatter.2.cloned.1.call-start = ((), (), s32[]{:S(2)}) async-start(), calls=%async_computation.1 | async-start | bytes 23592960 | tf_op jit(solution)/shard_map/reduce_scatter | solution.py:140
  7.2 51.8 %collective-permute-start = (bf16[384,3072]{1,0:T(8,128)(2,1)}, bf16[384,3072]{1,0:T(8,128)(2,1)S(1)}, u32[]{:S(2)}, u32[]{:S(2)}) collective-permute-start(bf16[384,3072]{1,0:T(8,128)(2,1)} %param.11), channel_id=1, source_target_pairs={{0,1},{1,2},{2,3},{3,0},{4,5},{5,6},{6,7},{7,4},{8,9},{9,10},{10,1... | collective-permute-start | bytes 7077896 | tf_op jit(solution)/shard_map/ppermute | solution.py:26
  7.7 60.2 %collective-permute-start.1 = (bf16[384,3072]{1,0:T(8,128)(2,1)}, bf16[384,3072]{1,0:T(8,128)(2,1)}, u32[]{:S(2)}, u32[]{:S(2)}) collective-permute-start(bf16[384,3072]{1,0:T(8,128)(2,1)} %param.11), channel_id=1, source_target_pairs={{0,3},{1,0},{2,1},{3,2},{4,7},{5,4},{6,5},{7,6},{8,11},{9,8},{10,9... | collective-permute-start | bytes 7077896 | tf_op jit(solution)/shard_map/ppermute | solution.py:34
  59.0 28.4 %collective-permute-start.2 = (bf16[384,3072]{1,0:T(8,128)(2,1)S(1)}, bf16[384,3072]{1,0:T(8,128)(2,1)}, u32[]{:S(2)}, u32[]{:S(2)}) collective-permute-start(bf16[384,3072]{1,0:T(8,128)(2,1)S(1)} %collective-permute-done), channel_id=1, source_target_pairs={{0,1},{1,2},{2,3},{3,0},{4,5},{5,6},{6,7},{7,4},{8,9},{9,10},{10,1... | collective-permute-start | bytes 7077896 | tf_op jit(solution)/shard_map/ppermute | solution.py:26
  65.6 1.7 copy-start.9
  69.9 19.5 %copy-start.10 = (f32[1536]{0:T(1024)S(1)}, f32[1536]{0:T(1024)}, u32[]{:S(2)}) copy-start(f32[1536]{0:T(1024)} %param.9) | copy-start | bytes 18436
  69.9 19.5 %copy-start.11 = (f32[1536]{0:T(1024)S(1)}, f32[1536]{0:T(1024)}, u32[]{:S(2)}) copy-start(f32[1536]{0:T(1024)} %param.10) | copy-start | bytes 18436
  89.4 4.1 copy-start.5
  93.5 2.2 copy-start
  95.7 6.1 %collective-permute-start.3 = (bf16[31,1536]{1,0:T(8,128)(2,1)S(1)}, bf16[31,1536]{1,0:T(8,128)(2,1)S(1)}, u32[]{:S(2)}, u32[]{:S(2)}) collective-permute-start(bf16[31,1536]{1,0:T(8,128)(2,1)S(1)} %slice.462), channel_id=1, source_target_pairs={{0,1},{1,2},{2,3},{3,4},{4,5},{5,6},{6,7},{7,8},{8,9},{9,10},{10,1... | collective-permute-start | bytes 285704 | tf_op jit(solution)/shard_map/ppermute | solution.py:47
  111.5 36.8 %copy-start.12 = (f32[1536]{0:T(1024)S(1)}, f32[1536]{0:T(1024)}, u32[]{:S(2)}) copy-start(f32[1536]{0:T(1024)} %param.13) | copy-start | bytes 18436
  111.6 36.8 %copy-start.6 = (bf16[384,1536]{1,0:T(8,128)(2,1)S(1)}, bf16[384,1536]{1,0:T(8,128)(2,1)}, u32[]{:S(2)}) copy-start(bf16[384,1536]{1,0:T(8,128)(2,1)} %param.15) | copy-start | bytes 3538948
  111.6 36.8 %copy-start.13 = (f32[1536]{0:T(1024)S(1)}, f32[1536]{0:T(1024)}, u32[]{:S(2)}) copy-start(f32[1536]{0:T(1024)} %param.14) | copy-start | bytes 18436
  111.6 3.5 collective-permute-start.4
  115.1 4.1 collective-permute-start.5
  119.2 3.7 collective-permute-start.6
  122.9 3.8 collective-permute-start.7
  126.6 4.7 collective-permute-start.8
  131.6 1.2 collective-permute-start.9
  132.8 3.7 collective-permute-start.10
  136.5 3.7 collective-permute-start.11
  140.1 3.7 collective-permute-start.12
  143.8 4.5 collective-permute-start.13
  150.9 1.2 collective-permute-start.14
  150.9 3.0 collective-permute-start.19
  152.0 3.7 collective-permute-start.15
  153.8 3.7 collective-permute-start.20
  155.7 3.7 collective-permute-start.16
  157.5 3.8 collective-permute-start.21
  159.3 3.7 collective-permute-start.17
  161.3 4.7 collective-permute-start.22
  163.0 4.6 collective-permute-start.18
  165.9 4.6 collective-permute-start.23
  170.5 7.1 %copy-start.14 = (f32[1536]{0:T(1024)}, f32[1536]{0:T(1024)S(1)}, u32[]{:S(2)}) copy-start(f32[1536]{0:T(1024)S(1)} %add.433) | copy-start | bytes 18436
  177.6 1.4 copy-start.1
  179.0 3.3 collective-permute-start.24
  222.8 4.5 copy-start.7
  222.8 5.5 copy-start.3
  227.2 1.0 copy-start.8
  237.7 323.9 %all-reduce.2.cloned.1.call-start = ((), (), s32[]{:S(2)}) async-start(), calls=%async_computation.2 | async-start | bytes 9437184 | tf_op jit(solution)/shard_map/psum | solution.py:151
  385.2 1.5 collective-permute-start.25
  386.7 7.0 %collective-permute-start.26 = (f32[32,1536]{1,0:T(8,128)S(1)}, f32[32,1536]{1,0:T(8,128)S(1)}, u32[]{:S(2)}, u32[]{:S(2)}) collective-permute-start(f32[32,1536]{1,0:T(8,128)S(1)} %add.465), channel_id=1, source_target_pairs={{0,2},{1,3},{2,0},{3,1},{4,6},{5,7},{6,4},{7,5},{8,10},{9,11},{10,... | collective-permute-start | bytes 589832 | tf_op jit(solution)/shard_map/ppermute | solution.py:57
  393.7 45.8 %copy-start.4 = (bf16[384,1536]{1,0:T(8,128)(2,1)S(1)}, bf16[384,1536]{1,0:T(8,128)(2,1)}, u32[]{:S(2)}) copy-start(bf16[384,1536]{1,0:T(8,128)(2,1)} %param.8) | copy-start | bytes 3538948
  393.8 21.3 %collective-permute-start.27 = (f32[32,1536]{1,0:T(8,128)S(1)}, f32[32,1536]{1,0:T(8,128)S(1)}, u32[]{:S(2)}, u32[]{:S(2)}) collective-permute-start(f32[32,1536]{1,0:T(8,128)S(1)} %add.466), channel_id=1, source_target_pairs={{0,4},{1,5},{2,6},{3,7},{4,0},{5,1},{6,2},{7,3},{8,12},{9,13},{10,... | collective-permute-start | bytes 589832 | tf_op jit(solution)/shard_map/ppermute | solution.py:57
  404.4 1.2 collective-permute-start.30
  404.5 1.7 collective-permute-start.35
  405.7 3.7 collective-permute-start.31
  406.2 3.7 collective-permute-start.36
  409.3 3.7 collective-permute-start.32
  409.9 4.6 collective-permute-start.37
  413.0 5.8 %collective-permute-start.33 = (f32[1536]{0:T(1024)S(1)}, f32[1536]{0:T(1024)S(1)}, u32[]{:S(2)}, u32[]{:S(2)}) collective-permute-start(f32[1536]{0:T(1024)S(1)} %add.472), channel_id=1, source_target_pairs={{0,8},{1,9},{2,10},{3,11},{4,12},{5,13},{6,14},{7,15},{8,0},{9,1},... | collective-permute-start | bytes 18440 | tf_op jit(solution)/shard_map/ppermute | solution.py:57
  414.5 4.8 collective-permute-start.38
  415.1 23.9 %collective-permute-start.28 = (f32[32,1536]{1,0:T(8,128)S(1)}, f32[32,1536]{1,0:T(8,128)S(1)}, u32[]{:S(2)}, u32[]{:S(2)}) collective-permute-start(f32[32,1536]{1,0:T(8,128)S(1)} %add.467), channel_id=1, source_target_pairs={{0,8},{1,9},{2,10},{3,11},{4,12},{5,13},{6,14},{7,15},{8,0},{9,1},... | collective-permute-start | bytes 589832 | tf_op jit(solution)/shard_map/ppermute | solution.py:57
  418.8 22.5 %collective-permute-start.34 = (f32[1536]{0:T(1024)S(1)}, f32[1536]{0:T(1024)S(1)}, u32[]{:S(2)}, u32[]{:S(2)}) collective-permute-start(f32[1536]{0:T(1024)S(1)} %add.473), channel_id=1, source_target_pairs={{0,16},{1,17},{2,18},{3,19},{4,20},{5,21},{6,22},{7,23},{8,24},{9,... | collective-permute-start | bytes 18440 | tf_op jit(solution)/shard_map/ppermute | solution.py:57
  419.3 22.6 %collective-permute-start.39 = (f32[1536]{0:T(1024)S(1)}, f32[1536]{0:T(1024)S(1)}, u32[]{:S(2)}, u32[]{:S(2)}) collective-permute-start(f32[1536]{0:T(1024)S(1)} %add.478), channel_id=1, source_target_pairs={{0,16},{1,17},{2,18},{3,19},{4,20},{5,21},{6,22},{7,23},{8,24},{9,... | collective-permute-start | bytes 18440 | tf_op jit(solution)/shard_map/ppermute | solution.py:57
  438.9 13.4 %collective-permute-start.29 = (f32[32,1536]{1,0:T(8,128)S(1)}, f32[32,1536]{1,0:T(8,128)S(1)}, u32[]{:S(2)}, u32[]{:S(2)}) collective-permute-start(f32[32,1536]{1,0:T(8,128)S(1)} %add.468), channel_id=1, source_target_pairs={{0,16},{1,17},{2,18},{3,19},{4,20},{5,21},{6,22},{7,23},{8,24},{9,... | collective-permute-start | bytes 589832 | tf_op jit(solution)/shard_map/ppermute | solution.py:57
Sparse Core Ops, SparseCore 0:
  237.8 141.0 reduce-scatter.1
  382.9 178.5 all-reduce.1
